TPU v7x, 256 devices: a whole 4x4x8 slice. The times are simulated.
256 devices in a mesh: dp: 32 (over z, x), seq: 8 (over y, core).
Axes of the slice: x: 4, y: 4, z: 8, core: 2. Of those that a mesh axis runs over, the one named last changes fastest.
Arguments:
- hidden: bfloat16 [32, 6144, 2560], P('dp', 'seq'), may hold values from -6 to 6
- log_decay: float32 [32, 40, 6144], P('dp', None, 'seq'), may hold values from -2 to 0, as said below
- input_weight: bfloat16 [2816, 2560], P(('dp', 'seq')), may hold values from -0.125 to 0.125
- conv_weight: bfloat16 [4, 2816], replicated, may hold values from -3 to 3
- conv_bias: float32 [2816], replicated, may hold values from -0.5 to 0.5
- skip_gain: float32 [40], replicated, may hold values from 0.5 to 1.5
Outputs:
- mixer_out: bfloat16 [32, 6144, 2560], P('dp', 'seq')
Inputs may be any that keep to these rules, and one draw needn't show every extreme that they name: `log_decay`: every value is negative.
All inputs are finite; a program needn't handle non-finite values.
Results may differ from a plain program's by a relative error of at most 0.0064.
Values may be sent and summed in bfloat16 or wider, within the bound.
No kernel may reach another device: no remote copies, remote signals or barrier semaphores. Data moves between devices by JAX's collectives and lax.ppermute only.
A program may use at most 128 MiB of HBM per device.

v0:
```python
import jax
import jax.numpy as jnp
from jax import lax
from jax.sharding import Mesh, PartitionSpec as P

HALF_HEADS = 40
HEAD_DIM = 64
STATE = 128
SPAN = 256
CONV = 4
INNER = 2560
COLS = 2816


def mixing_output(x_heads, b_span, c_span, cumulative, step_size):
    scores = jnp.dot(c_span, b_span.T, preferred_element_type=jnp.float32)
    span_len = cumulative.shape[1]
    causal = jnp.arange(span_len)[:, None] >= jnp.arange(span_len)[None, :]
    spread = jnp.where(causal[None], cumulative[:, :, None] - cumulative[:, None, :], -jnp.inf)
    mixing = (scores[None] * jnp.exp(spread) * step_size[:, None, :]).astype(jnp.bfloat16)
    return jnp.einsum("hqk,khp->qhp", mixing, x_heads, preferred_element_type=jnp.float32)


def span_state(x_heads, b_span, cumulative, step_size):
    weight = jnp.exp(cumulative[:, -1:] - cumulative) * step_size
    decayed = (x_heads * weight.T[:, :, None]).astype(jnp.bfloat16)
    return jnp.einsum("khp,kn->hpn", decayed, b_span, preferred_element_type=jnp.float32)


def state_output(c_span, entering, cumulative):
    readout = jnp.einsum(
        "qn,hpn->qhp", c_span.astype(jnp.float32), entering, precision=lax.Precision.HIGHEST
    )
    return jnp.exp(cumulative).T[:, :, None] * readout


SEQ = ("y", "core")


def shifted(array, by):
    peers = lax.axis_size(SEQ)
    pairs = [(i, i + by) for i in range(peers) if i + by < peers]
    return lax.ppermute(array, SEQ, pairs)


def scan_entering(total, state):
    acc_total, acc_state = (shifted(total, 1), shifted(state, 1))
    by = 1
    while by < lax.axis_size(SEQ):
        got_total, got_state = (shifted(acc_total, by), shifted(acc_state, by))
        acc_state = jnp.exp(acc_total)[:, None, None] * got_state + acc_state
        acc_total = acc_total + got_total
        by *= 2
    return acc_state


def project(token_rows, input_weight):
    rows = input_weight.shape[0]
    mine = lax.all_gather(input_weight, ("dp", "y"), axis=0, tiled=True)
    other = lax.ppermute(mine, "core", [(0, 1), (1, 0)])
    dims = (((1,), (1,)), ((), ()))
    p_mine = lax.dot_general(token_rows, mine, dims, preferred_element_type=jnp.float32).astype(
        jnp.bfloat16
    )
    p_other = lax.dot_general(token_rows, other, dims, preferred_element_type=jnp.float32).astype(
        jnp.bfloat16
    )
    first = lax.axis_index("core") == 0
    p0 = jnp.where(first, p_mine, p_other)
    p1 = jnp.where(first, p_other, p_mine)
    length = token_rows.shape[0]
    groups = mine.shape[0] // rows
    return jnp.stack(
        [p0.reshape(length, groups, rows), p1.reshape(length, groups, rows)], axis=2
    ).reshape(length, COLS)


def body(hidden, log_decay, input_weight, conv_weight, conv_bias, skip_gain):
    token_rows = hidden[0]
    length = token_rows.shape[0]
    projected = project(token_rows, input_weight)
    last_rows = projected[length - (CONV - 1) :]
    before_rows = shifted(last_rows, 1)
    extended = jnp.concatenate([before_rows, projected], axis=0)
    filtered = jnp.broadcast_to(conv_bias[None, :], (length, COLS))
    for kernel_tap in range(CONV):
        filtered = (
            filtered
            + extended[kernel_tap : kernel_tap + length].astype(jnp.float32)
            * conv_weight[kernel_tap].astype(jnp.float32)[None, :]
        )
    active = jax.nn.silu(filtered).astype(jnp.bfloat16)
    span_count = length // SPAN
    x_all = active[:, :INNER].reshape(span_count, SPAN, HALF_HEADS, HEAD_DIM)
    b_all = active[:, INNER : INNER + STATE].reshape(span_count, SPAN, STATE)
    c_all = active[:, INNER + STATE :].reshape(span_count, SPAN, STATE)
    decay_spans = log_decay[0].reshape(HALF_HEADS, span_count, SPAN).transpose(1, 0, 2)
    cumulative = jnp.cumsum(decay_spans, axis=2)
    steps_all = -decay_spans
    totals = cumulative[:, :, -1]
    device_total = jnp.sum(totals, axis=0)
    zero_state = jnp.zeros((HALF_HEADS, HEAD_DIM, STATE), jnp.float32)

    def state_of(inputs):
        x_heads, b_span, cum_span, step_span = inputs
        return span_state(x_heads, b_span, cum_span, step_span)

    states = lax.map(state_of, (x_all, b_all, cumulative, steps_all))

    def gather_local(held_state, inputs):
        span_total, state_piece = inputs
        return (jnp.exp(span_total)[:, None, None] * held_state + state_piece, None)

    local_end, _ = lax.scan(gather_local, zero_state, (totals, states))
    entering_dev = scan_entering(device_total, local_end)

    def emit(held_state, inputs):
        x_heads, b_span, c_span, cum_span, step_span, span_total, state_piece = inputs
        outputs = mixing_output(x_heads, b_span, c_span, cum_span, step_span) + state_output(
            c_span, held_state, cum_span
        )
        return (jnp.exp(span_total)[:, None, None] * held_state + state_piece, outputs)

    _, outputs = lax.scan(
        emit, entering_dev, (x_all, b_all, c_all, cumulative, steps_all, totals, states)
    )
    outputs = outputs.reshape(length, HALF_HEADS, HEAD_DIM)
    final = outputs + skip_gain[None, :, None] * x_all.reshape(length, HALF_HEADS, HEAD_DIM).astype(
        jnp.float32
    )
    return final.reshape(1, length, INNER).astype(jnp.bfloat16)


def solution(mesh):
    split = Mesh(
        mesh.devices.reshape(mesh.shape["dp"], mesh.shape["seq"] // 2, 2), ("dp", "y", "core")
    )
    placed = (P("dp", SEQ, None), P("dp", None, SEQ), P(("dp",) + SEQ, None), P(), P(), P())
    return jax.shard_map(
        body, mesh=split, in_specs=placed, out_specs=P("dp", SEQ, None), check_vma=False
    )
```

profile of v0, /device:TPU:8, one launch (start us, length us, event | category | flops | bytes accessed | tf_op | source)
XLA Modules:
  0.0 609.2 jit_solution(4100899505798613028)
XLA Ops:
  7.3 136.0 %all-gather.3.cloned.1.call-done = bf16[128,11,2560]{2,1,0:T(8,128)(2,1)} async-done(((bf16[1,11,2560]{2,1,0:T(8,128)(2,1)}), bf16[128,11,2560]{2,1,0:T(8,128)(2,1)}) %all-gather.3.cloned.1.call-update) | async-done | bytes 7208976 | tf_op jit(solution)/shard_map/all_gather | solution.py:59
  143.3 13.2 %reshape.82 = bf16[1408,2560]{1,0:T(8,128)(2,1)} reshape(bf16[128,11,2560]{2,1,0:T(8,128)(2,1)} %all-gather.3.cloned.1.call-done) | data formatting | bytes 14417920
  158.9 10.3 %fusion.40 = bf16[768,1408]{1,0:T(8,128)(2,1)S(1)} fusion(bf16[1408,2560]{1,0:T(8,128)(2,1)} %reshape.82, bf16[1,768,2560]{2,1,0:T(8,128)(2,1)} %param.12), kind=kOutput, calls=%fused_computation.64 | convolution fusion | flops 5537562624 | bytes 13303808 | tf_op jit(solution)/shard_map/dot_general | solution.py:62
  169.3 10.6 %broadcast_select_fusion = (bf16[768,1408]{1,0:T(8,128)(2,1)}, bf16[768,1408]{1,0:T(8,128)(2,1)S(1)}) fusion(bf16[768,1408]{1,0:T(8,128)(2,1)S(1)} %fusion.40, pred[]{:T(512)S(6)} %eq.3, bf16[1408,2560]{1,0:T(8,128)(2,1)} %collective-permute-done.3, bf16[1,768,2560]{2,1,0:T(8,128)(2,1)S(1)} %copy-done.5), kind=kOutput, calls=%fused_computation.66 | convolution fusion | flops 5539725312 | bytes 17629184 | tf_op jit(solution)/shard_map/dot_general | solution.py:65
  186.9 4.2 copy.57
  202.5 6.4 %copy.59 = bf16[768,128,2,11]{0,3,2,1:T(8,128)(2,1)} copy(bf16[768,128,2,11]{0,3,1,2:T(8,128)(2,1)} %constant_dynamic-update-slice_fusion) | data formatting | bytes 8650752 | tf_op jit(solution)/shard_map/stack | solution.py:73
  208.9 7.7 %reshape.72 = bf16[768,2816]{0,1:T(8,128)(2,1)} reshape(bf16[768,128,2,11]{0,3,2,1:T(8,128)(2,1)} %copy.59) | data formatting | bytes 8650752 | tf_op jit(solution)/shard_map/reshape | solution.py:75
  217.0 15.4 %multiply_convert_fusion.5 = bf16[768,2816]{0,1:T(8,128)(2,1)S(1)} fusion(bf16[768,2816]{0,1:T(8,128)(2,1)} %reshape.72, bf16[3,2816]{0,1:T(8,128)(2,1)S(1)} %copy.60, f32[2816]{0:T(1024)S(1)} %get-tuple-element.197, f32[2816]{0:T(1024)S(1)} %get-tuple-element.198, f32[2816]{0:T(1024)S(1)} %get-tuple-element.196, f32[2816]{0:T(1024)S(1)} %get-tuple-element.195, ...), kind=kLoop, calls=%fused_computation.50 | loop fusion | flops 56229888 | bytes 8723968 | tf_op jit(solution)/shard_map/convert_element_type | solution.py:92
  235.9 11.3 %reshape.73 = bf16[3,256,40,64]{1,0,3,2:T(4,128)(2,1)} reshape(bf16[768,2560]{0,1:T(8,128)(2,1)} %slice.72) | data formatting | bytes 7864320 | tf_op jit(solution)/shard_map/reshape | solution.py:94
  247.2 5.2 copy.62
  252.4 9.8 %while.33 = (s32[]{:T(128)}, f32[3,40,64,128]{3,2,1,0:T(8,128)}, bf16[3,256,40,64]{1,3,2,0:T(8,128)(2,1)}, f32[3,40,256]{2,1,0:T(8,128)S(1)}, f32[3,40,256]{2,0,...) while((s32[]{:T(128)}, f32[3,40,64,128]{3,2,1,0:T(8,128)}, bf16[3,256,40,64]{1,3,2,0:T(8,128)(2,1)}, ...), condition=%wide.region_4.5_spmd, body=%wide.region_3.4_spmd.sunk | while | flops 169758720 | bytes 3262517 | solution.py:108
  262.2 4.7 while.35
  266.9 3.0 collective-permute-start.5
  269.9 15.9 %collective-permute-done.5 = f32[40,64,128]{2,1,0:T(8,128)S(1)} collective-permute-done((f32[40,64,128]{2,1,0:T(8,128)S(1)}, f32[40,64,128]{2,1,0:T(8,128)S(1)}, u32[]{:S(2)}, u32[]{:S(2)}) %collective-permute-start.5) | collective-permute-done | bytes 1310752 | tf_op jit(solution)/shard_map/ppermute | solution.py:43
  287.7 3.5 collective-permute-start
  291.2 13.5 %collective-permute-done = f32[40]{0:T(128)S(1)} collective-permute-done((f32[40]{0:T(128)S(1)}, f32[40]{0:T(128)S(1)}, u32[]{:S(2)}, u32[]{:S(2)}) %collective-permute-start) | collective-permute-done | bytes 192 | tf_op jit(solution)/shard_map/ppermute | solution.py:43
  309.9 3.4 collective-permute-start.7
  313.3 28.5 %collective-permute-done.7 = f32[40,64,128]{2,1,0:T(8,128)S(1)} collective-permute-done((f32[40,64,128]{2,1,0:T(8,128)S(1)}, f32[40,64,128]{2,1,0:T(8,128)S(1)}, u32[]{:S(2)}, u32[]{:S(2)}) %collective-permute-start.7) | collective-permute-done | bytes 1310752 | tf_op jit(solution)/shard_map/ppermute | solution.py:43
  347.3 26.7 %collective-permute-done.2 = f32[40]{0:T(128)S(1)} collective-permute-done((f32[40]{0:T(128)S(1)}, f32[40]{0:T(128)S(1)}, u32[]{:S(2)}, u32[]{:S(2)}) %collective-permute-start.2) | collective-permute-done | bytes 192 | tf_op jit(solution)/shard_map/ppermute | solution.py:43
  376.3 209.5 %while.34 = (s32[]{:T(128)}, f32[40,64,128]{2,1,0:T(8,128)}, f32[3,256,40,64]{1,0,3,2:T(4,128)}, f32[3,40]{1,0:T(4,128)S(1)}, f32[3,40,64,128]{3,2,1,0:T(8,128)}...) while((s32[]{:T(128)}, f32[40,64,128]{2,1,0:T(8,128)}, ...), condition=%wide.region_8.9_spmd, body=%wide.region_7.8_spmd.sunk | while | flops 1374093312 | bytes 26208364 | solution.py:124
  379.2 4.3 fusion.76
  386.4 56.8 %dynamic_update_slice.12 = f32[3,256,40,64]{1,0,3,2:T(4,128)} dynamic-update-slice(f32[3,256,40,64]{1,0,3,2:T(4,128)} %get-tuple-element.428, f32[1,256,40,64]{1,0,3,2:T(1,128)S(1)} %copy.94, s32[]{:T(128)} %get-tuple-element.426, s32[]{:T(128)} %constant.52.clone.1..sunk, s32[]{:T(128)} %constant.52.clone.1..sunk, s32[]{:T(128)} %constant.52.clone.1..sunk) | dynamic-update-slice | bytes 5242884 | tf_op jit(solution)/shard_map/while/body/jit(dynamic_update_index_in_dim)/dynamic_update_slice | solution.py:124
  443.2 3.0 bitcast_add_fusion.5
  449.0 4.3 fusion.76
  456.2 56.8 %dynamic_update_slice.12 = f32[3,256,40,64]{1,0,3,2:T(4,128)} dynamic-update-slice(f32[3,256,40,64]{1,0,3,2:T(4,128)} %get-tuple-element.428, f32[1,256,40,64]{1,0,3,2:T(1,128)S(1)} %copy.94, s32[]{:T(128)} %get-tuple-element.426, s32[]{:T(128)} %constant.52.clone.1..sunk, s32[]{:T(128)} %constant.52.clone.1..sunk, s32[]{:T(128)} %constant.52.clone.1..sunk) | dynamic-update-slice | bytes 5242884 | tf_op jit(solution)/shard_map/while/body/jit(dynamic_update_index_in_dim)/dynamic_update_slice | solution.py:124
  513.0 3.0 bitcast_add_fusion.5
  518.8 4.3 fusion.76
  526.1 56.8 %dynamic_update_slice.12 = f32[3,256,40,64]{1,0,3,2:T(4,128)} dynamic-update-slice(f32[3,256,40,64]{1,0,3,2:T(4,128)} %get-tuple-element.428, f32[1,256,40,64]{1,0,3,2:T(1,128)S(1)} %copy.94, s32[]{:T(128)} %get-tuple-element.426, s32[]{:T(128)} %constant.52.clone.1..sunk, s32[]{:T(128)} %constant.52.clone.1..sunk, s32[]{:T(128)} %constant.52.clone.1..sunk) | dynamic-update-slice | bytes 5242884 | tf_op jit(solution)/shard_map/while/body/jit(dynamic_update_index_in_dim)/dynamic_update_slice | solution.py:124
  582.8 3.0 bitcast_add_fusion.5
  585.8 5.9 copy.81
  591.8 4.3 fusion.35
  596.0 6.3 %copy.69 = bf16[1,768,2560]{2,1,0:T(8,128)(2,1)} copy(bf16[1,768,2560]{1,2,0:T(8,128)(2,1)} %fusion.35) | data formatting | bytes 7864320 | tf_op jit(solution)/shard_map/convert_element_type | solution.py:131
  (113 shorter events, 71.8 us)
Async XLA Ops:
  6.5 136.7 %all-gather.3.cloned.1.call-start = ((), (), s32[]{:S(2)}) async-start(), calls=%async_computation | async-start | bytes 10567680 | tf_op jit(solution)/shard_map/all_gather | solution.py:59
  7.3 149.2 %copy-start.1 = (f32[1,40,768]{2,1,0:T(8,128)S(1)}, f32[1,40,768]{2,1,0:T(8,128)}, u32[]{:S(2)}) copy-start(f32[1,40,768]{2,1,0:T(8,128)} %param.13) | copy-start | bytes 368644
  7.3 151.4 %copy-start.2 = (bf16[4,2816]{1,0:T(4,128)(2,1)S(1)}, bf16[4,2816]{1,0:T(4,128)(2,1)}, u32[]{:S(2)}) copy-start(bf16[4,2816]{1,0:T(4,128)(2,1)} %param.15) | copy-start | bytes 67588
  156.4 12.8 %collective-permute-start.3 = (bf16[1408,2560]{1,0:T(8,128)(2,1)}, bf16[1408,2560]{1,0:T(8,128)(2,1)}, u32[]{:S(2)}, u32[]{:S(2)}) collective-permute-start(bf16[1408,2560]{1,0:T(8,128)(2,1)} %reshape.82), channel_id=1, source_target_pairs={{0,1},{1,0},{2,3},{3,2},{4,5},{5,4},{6,7},{7,6},{8,9},{9,8},{10,11... | collective-permute-start | bytes 21626888 | tf_op jit(solution)/shard_map/ppermute | solution.py:60
  158.9 10.3 %copy-start.5 = (bf16[1,768,2560]{2,1,0:T(8,128)(2,1)S(1)}, bf16[1,768,2560]{2,1,0:T(8,128)(2,1)}, u32[]{:S(2)}) copy-start(bf16[1,768,2560]{2,1,0:T(8,128)(2,1)} %param.12) | copy-start | bytes 11796484
  199.7 17.0 %collective-permute-start.4 = (bf16[3,2816]{1,0:T(4,128)(2,1)S(1)}, bf16[3,2816]{1,0:T(4,128)(2,1)S(1)}, u32[]{:S(2)}, u32[]{:S(2)}) collective-permute-start(bf16[3,2816]{1,0:T(4,128)(2,1)S(1)} %slice.52), channel_id=1, source_target_pairs={{0,1},{1,2},{2,3},{3,4},{4,5},{5,6},{6,7},{8,9},{9,10},{10,11},{11... | collective-permute-start | bytes 50696 | tf_op jit(solution)/shard_map/ppermute | solution.py:43
  208.9 8.1 %copy-start.3 = (f32[2816]{0:T(1024)S(1)}, f32[2816]{0:T(1024)}, u32[]{:S(2)}) copy-start(f32[2816]{0:T(1024)} %param.16) | copy-start | bytes 33796
  232.4 3.3 copy-start
  266.9 18.9 %collective-permute-start.5 = (f32[40,64,128]{2,1,0:T(8,128)S(1)}, f32[40,64,128]{2,1,0:T(8,128)S(1)}, u32[]{:S(2)}, u32[]{:S(2)}) collective-permute-start(f32[40,64,128]{2,1,0:T(8,128)S(1)} %get-tuple-element.112), channel_id=1, source_target_pairs={{0,1},{1,2},{2,3},{3,4},{4,5},{5,6},{6,7},{8,9},{9,10},{10,11},{11... | collective-permute-start | bytes 3932168 | tf_op jit(solution)/shard_map/ppermute | solution.py:43
  285.8 23.8 %collective-permute-start.6 = (f32[40,64,128]{2,1,0:T(8,128)S(1)}, f32[40,64,128]{2,1,0:T(8,128)S(1)}, u32[]{:S(2)}, u32[]{:S(2)}) collective-permute-start(f32[40,64,128]{2,1,0:T(8,128)S(1)} %collective-permute-done.5), channel_id=1, source_target_pairs={{0,1},{1,2},{2,3},{3,4},{4,5},{5,6},{6,7},{8,9},{9,10},{10,11},{11... | collective-permute-start | bytes 3932168 | tf_op jit(solution)/shard_map/ppermute | solution.py:43
  287.7 17.1 %collective-permute-start = (f32[40]{0:T(128)S(1)}, f32[40]{0:T(128)S(1)}, u32[]{:S(2)}, u32[]{:S(2)}) collective-permute-start(f32[40]{0:T(128)S(1)} %get-tuple-element.193), channel_id=1, source_target_pairs={{0,1},{1,2},{2,3},{3,4},{4,5},{5,6},{6,7},{8,9},{9,10},{10,11},{11... | collective-permute-start | bytes 488 | tf_op jit(solution)/shard_map/ppermute | solution.py:43
  304.8 4.8 collective-permute-start.1
  309.6 37.5 %copy-start.4 = (f32[40]{0:T(128)S(1)}, f32[40]{0:T(128)}, u32[]{:S(2)}) copy-start(f32[40]{0:T(128)} %param.17) | copy-start | bytes 484
  309.9 31.9 %collective-permute-start.7 = (f32[40,64,128]{2,1,0:T(8,128)S(1)}, f32[40,64,128]{2,1,0:T(8,128)S(1)}, u32[]{:S(2)}, u32[]{:S(2)}) collective-permute-start(f32[40,64,128]{2,1,0:T(8,128)S(1)} %multiply_add_fusion.2), channel_id=1, source_target_pairs={{0,2},{1,3},{2,4},{3,5},{4,6},{5,7},{8,10},{9,11},{10,12},{11,13},... | collective-permute-start | bytes 3932168 | tf_op jit(solution)/shard_map/ppermute | solution.py:43
  342.0 33.0 %collective-permute-start.8 = (f32[40,64,128]{2,1,0:T(8,128)S(1)}, f32[40,64,128]{2,1,0:T(8,128)S(1)}, u32[]{:S(2)}, u32[]{:S(2)}) collective-permute-start(f32[40,64,128]{2,1,0:T(8,128)S(1)} %multiply_add_fusion.1), channel_id=1, source_target_pairs={{0,4},{1,5},{2,6},{3,7},{8,12},{9,13},{10,14},{11,15},{16,20},{17,... | collective-permute-start | bytes 3932168 | tf_op jit(solution)/shard_map/ppermute | solution.py:43
  345.0 29.0 %collective-permute-start.2 = (f32[40]{0:T(128)S(1)}, f32[40]{0:T(128)S(1)}, u32[]{:S(2)}, u32[]{:S(2)}) collective-permute-start(f32[40]{0:T(128)S(1)} %get-tuple-element.242), channel_id=1, source_target_pairs={{0,2},{1,3},{2,4},{3,5},{4,6},{5,7},{8,10},{9,11},{10,12},{11,13},... | collective-permute-start | bytes 488 | tf_op jit(solution)/shard_map/ppermute | solution.py:43
Sparse Core Ops, SparseCore 0:
  10.8 132.3 all-gather.2
where the time goes:
time: 615 us; the launch traced here: 609 us
  local copies, waits for them, and re-layouts  262 us (43%)
  waiting for transfers between devices  224 us (36%)
  matrix products  50.5 us (8%)
  other arithmetic  37.4 us (6%)
  starting transfers between devices  21.4 us (3%)
  between operations  13.7 us (2%)
    dynamic_update_slice x6, local copies, waits for them, and re-layouts, body(): lax.scan(emit, entering_dev, (x_all, b_all, c_all, cumulative, steps_all,...  179 us
    all_gather x1, waiting for transfers between devices, project(): mine = lax.all_gather(input_weight, ('dp', 'y'), axis=0, tiled=True)  136 us
    ppermute x8, waiting for transfers between devices, shifted(): return lax.ppermute(array, SEQ, pairs)  87.6 us
    ppermute x8, starting transfers between devices, shifted(): return lax.ppermute(array, SEQ, pairs)  21.4 us
    unnamed x15, local copies, waits for them, and re-layouts  21 us
    convert_element_type x1, other arithmetic, body(): active = jax.nn.silu(filtered).astype(jnp.bfloat16)  15.4 us
    another operation x4, local copies, waits for them, and re-layouts, project(): jnp.stack([p0.reshape(length, groups, rows), p1.reshape(length, groups, r...  13.8 us
    dot_general x3, matrix products, mixing_output(): jnp.einsum('hqk,khp->qhp', mixing, x_heads, preferred_element_type=jnp.fl...  12.8 us
  transfers between devices with their start and end apart: 10, of which 6 were waited for; matrix products, arithmetic and copies ran while one was open for 5% of the time, Pallas kernels for 0%

commit v1 on v0

--- a/solution.py
+++ b/solution.py
@@ -1,3 +1,4 @@
+import functools
 import jax
 import jax.numpy as jnp
 from jax import lax
@@ -10,6 +11,15 @@
 CONV = 4
 INNER = 2560
 COLS = 2816
+
+
+def _save_results(target, row_axis):
+    return jnp.concatenate(
+        lax.all_to_all(jnp.stack([target] * lax.psum(1, row_axis), 0), row_axis, 0, 0), 0
+    )
+
+
+recover_skins = functools.partial(_save_results, row_axis=("dp", "y"))
 
 
 def mixing_output(x_heads, b_span, c_span, cumulative, step_size):
@@ -56,7 +66,7 @@
 
 def project(token_rows, input_weight):
     rows = input_weight.shape[0]
-    mine = lax.all_gather(input_weight, ("dp", "y"), axis=0, tiled=True)
+    mine = recover_skins(input_weight)
     other = lax.ppermute(mine, "core", [(0, 1), (1, 0)])
     dims = (((1,), (1,)), ((), ()))
     p_mine = lax.dot_general(token_rows, mine, dims, preferred_element_type=jnp.float32).astype(

time: 615 us -> 716 us (1.16)
  blocking collectives: 0 us -> 247 us
  waiting for transfers between devices: 224 us -> 91.2 us
  between operations: 13.7 us -> 0.3 us
    all_to_all x0 -> x1, blocking collectives: none -> 247 us  [_save_results(): lax.all_to_all(jnp.stack([target] * lax.psum(1, row_axis), 0), row_axis,...]
    all_gather x1 -> x0, waiting for transfers between devices: 136 us -> none  [project(): mine = lax.all_gather(input_weight, ('dp', 'y'), axis=0, tiled=True)]
    reshape x2 -> x3, local copies, waits for them, and re-layouts: 0.12 us -> 13.3 us  [the longest x1 13.2 us: _save_results(): jnp.concatenate(lax.all_to_all(jnp.stack([target] * lax.psum(1, row_axis)...]
    unnamed x15 -> x14, local copies, waits for them, and re-layouts: 21 us -> 7.85 us
  transfers between devices with their start and end apart: 10 -> 9, of which waited for: 6 -> 5; matrix products, arithmetic and copies ran while one was open for 5% -> 4% of each run, Pallas kernels for 0% -> 0%
where the time goes in v1:
time: 716 us; the launch traced here: 709 us
  local copies, waits for them, and re-layouts  264 us (37%)
  blocking collectives  247 us (34%)
  waiting for transfers between devices  91.2 us (13%)
  matrix products  50.5 us (7%)
  other arithmetic  37.4 us (5%)
  starting transfers between devices  18.8 us (3%)
    all_to_all x1, blocking collectives, _save_results(): lax.all_to_all(jnp.stack([target] * lax.psum(1, row_axis), 0), row_axis,...  247 us
    dynamic_update_slice x6, local copies, waits for them, and re-layouts, body(): lax.scan(emit, entering_dev, (x_all, b_all, c_all, cumulative, steps_all,...  179 us
    ppermute x8, waiting for transfers between devices, shifted(): return lax.ppermute(array, SEQ, pairs)  91.2 us
    ppermute x8, starting transfers between devices, shifted(): return lax.ppermute(array, SEQ, pairs)  18.8 us
    convert_element_type x1, other arithmetic, body(): active = jax.nn.silu(filtered).astype(jnp.bfloat16)  15.4 us
  transfers between devices with their start and end apart: 9, of which 5 were waited for; matrix products, arithmetic and copies ran while one was open for 4% of the time, Pallas kernels for 0%

profile of v1, /device:TPU:8, one launch (start us, length us, event | category | flops | bytes accessed | tf_op | source)
XLA Modules:
  0.0 709.3 jit_solution(8490689134180259980)
XLA Ops:
  2.2 247.1 %all_to_all.5 = bf16[128,11,2560]{2,1,0:T(8,128)(2,1)} all-to-all(bf16[128,11,2560]{2,1,0:T(8,128)(2,1)S(1)} %stack.4), channel_id=1, replica_groups=mesh['dp'=32,'y'=4,'core'=2] {'dp','y'}, dimensions={0} | all-to-all | bytes 14417920 | tf_op jit(solution)/shard_map/all_to_all | solution.py:18
  249.3 13.2 %reshape.77 = bf16[1408,2560]{1,0:T(8,128)(2,1)} reshape(bf16[128,11,2560]{2,1,0:T(8,128)(2,1)} %all_to_all.5) | data formatting | bytes 14417920 | tf_op jit(solution)/shard_map/reshape | solution.py:17
  265.0 10.3 %fusion.40 = bf16[768,1408]{1,0:T(8,128)(2,1)S(1)} fusion(bf16[1408,2560]{1,0:T(8,128)(2,1)} %reshape.77, bf16[1,768,2560]{2,1,0:T(8,128)(2,1)} %param.12), kind=kOutput, calls=%fused_computation.64 | convolution fusion | flops 5537562624 | bytes 13303808 | tf_op jit(solution)/shard_map/dot_general | solution.py:72
  275.4 10.6 %broadcast_select_fusion = (bf16[768,1408]{1,0:T(8,128)(2,1)}, bf16[768,1408]{1,0:T(8,128)(2,1)S(1)}) fusion(bf16[768,1408]{1,0:T(8,128)(2,1)S(1)} %fusion.40, pred[]{:T(512)S(6)} %eq.3, bf16[1408,2560]{1,0:T(8,128)(2,1)} %collective-permute-done.3, bf16[1,768,2560]{2,1,0:T(8,128)(2,1)S(1)} %copy-done.5), kind=kOutput, calls=%fused_computation.66 | convolution fusion | flops 5539725312 | bytes 17629184 | tf_op jit(solution)/shard_map/dot_general | solution.py:75
  293.1 4.1 copy.39
  308.6 6.4 copy.41
  315.0 7.7 %reshape.78 = bf16[768,2816]{0,1:T(8,128)(2,1)} reshape(bf16[768,128,2,11]{0,3,2,1:T(8,128)(2,1)} %copy.41) | data formatting | bytes 8650752 | tf_op jit(solution)/shard_map/reshape | solution.py:85
  323.1 15.4 %multiply_convert_fusion.5 = bf16[768,2816]{0,1:T(8,128)(2,1)S(1)} fusion(bf16[768,2816]{0,1:T(8,128)(2,1)} %reshape.78, bf16[3,2816]{0,1:T(8,128)(2,1)S(1)} %copy.42, f32[2816]{0:T(1024)S(1)} %get-tuple-element.181, f32[2816]{0:T(1024)S(1)} %get-tuple-element.182, f32[2816]{0:T(1024)S(1)} %get-tuple-element.180, f32[2816]{0:T(1024)S(1)} %get-tuple-element.179, ...), kind=kLoop, calls=%fused_computation.50 | loop fusion | flops 56229888 | bytes 8723968 | tf_op jit(solution)/shard_map/convert_element_type | solution.py:102
  342.0 11.3 %reshape.79 = bf16[3,256,40,64]{1,0,3,2:T(4,128)(2,1)} reshape(bf16[768,2560]{0,1:T(8,128)(2,1)} %slice.72) | data formatting | bytes 7864320 | tf_op jit(solution)/shard_map/reshape | solution.py:104
  353.2 5.2 copy.44
  358.4 9.8 %while.33 = (s32[]{:T(128)}, f32[3,40,64,128]{3,2,1,0:T(8,128)}, bf16[3,256,40,64]{1,3,2,0:T(8,128)(2,1)}, f32[3,40,256]{2,1,0:T(8,128)S(1)}, f32[3,40,256]{2,0,...) while((s32[]{:T(128)}, f32[3,40,64,128]{3,2,1,0:T(8,128)}, bf16[3,256,40,64]{1,3,2,0:T(8,128)(2,1)}, ...), condition=%wide.region_4.5_spmd, body=%wide.region_3.4_spmd.sunk | while | flops 169758720 | bytes 3262517 | solution.py:118
  368.2 4.7 while.35
  374.9 17.0 %collective-permute-done.5 = f32[40,64,128]{2,1,0:T(8,128)S(1)} collective-permute-done((f32[40,64,128]{2,1,0:T(8,128)S(1)}, f32[40,64,128]{2,1,0:T(8,128)S(1)}, u32[]{:S(2)}, u32[]{:S(2)}) %collective-permute-start.5) | collective-permute-done | bytes 1310752 | tf_op jit(solution)/shard_map/ppermute | solution.py:53
  396.0 14.8 %collective-permute-done = f32[40]{0:T(128)S(1)} collective-permute-done((f32[40]{0:T(128)S(1)}, f32[40]{0:T(128)S(1)}, u32[]{:S(2)}, u32[]{:S(2)}) %collective-permute-start) | collective-permute-done | bytes 192 | tf_op jit(solution)/shard_map/ppermute | solution.py:53
  418.1 28.6 %collective-permute-done.7 = f32[40,64,128]{2,1,0:T(8,128)S(1)} collective-permute-done((f32[40,64,128]{2,1,0:T(8,128)S(1)}, f32[40,64,128]{2,1,0:T(8,128)S(1)}, u32[]{:S(2)}, u32[]{:S(2)}) %collective-permute-start.7) | collective-permute-done | bytes 1310752 | tf_op jit(solution)/shard_map/ppermute | solution.py:53
  446.9 3.9 collective-permute-start.8
  453.1 27.8 %collective-permute-done.2 = f32[40]{0:T(128)S(1)} collective-permute-done((f32[40]{0:T(128)S(1)}, f32[40]{0:T(128)S(1)}, u32[]{:S(2)}, u32[]{:S(2)}) %collective-permute-start.2) | collective-permute-done | bytes 192 | tf_op jit(solution)/shard_map/ppermute | solution.py:53
  483.4 209.5 %while.34 = (s32[]{:T(128)}, f32[40,64,128]{2,1,0:T(8,128)}, f32[3,256,40,64]{1,0,3,2:T(4,128)}, f32[3,40]{1,0:T(4,128)S(1)}, f32[3,40,64,128]{3,2,1,0:T(8,128)}...) while((s32[]{:T(128)}, f32[40,64,128]{2,1,0:T(8,128)}, ...), condition=%wide.region_8.9_spmd, body=%wide.region_7.8_spmd.sunk | while | flops 1374093312 | bytes 26208364 | solution.py:134
  486.2 4.3 fusion.76
  490.5 2.9 copy.76
  493.4 56.8 %dynamic_update_slice.12 = f32[3,256,40,64]{1,0,3,2:T(4,128)} dynamic-update-slice(f32[3,256,40,64]{1,0,3,2:T(4,128)} %get-tuple-element.412, f32[1,256,40,64]{1,0,3,2:T(1,128)S(1)} %copy.76, s32[]{:T(128)} %get-tuple-element.410, s32[]{:T(128)} %constant.52.clone.1..sunk, s32[]{:T(128)} %constant.52.clone.1..sunk, s32[]{:T(128)} %constant.52.clone.1..sunk) | dynamic-update-slice | bytes 5242884 | tf_op jit(solution)/shard_map/while/body/jit(dynamic_update_index_in_dim)/dynamic_update_slice | solution.py:134
  550.2 3.0 bitcast_add_fusion.5
  556.0 4.3 fusion.76
  560.3 2.9 copy.76
  563.2 56.8 %dynamic_update_slice.12 = f32[3,256,40,64]{1,0,3,2:T(4,128)} dynamic-update-slice(f32[3,256,40,64]{1,0,3,2:T(4,128)} %get-tuple-element.412, f32[1,256,40,64]{1,0,3,2:T(1,128)S(1)} %copy.76, s32[]{:T(128)} %get-tuple-element.410, s32[]{:T(128)} %constant.52.clone.1..sunk, s32[]{:T(128)} %constant.52.clone.1..sunk, s32[]{:T(128)} %constant.52.clone.1..sunk) | dynamic-update-slice | bytes 5242884 | tf_op jit(solution)/shard_map/while/body/jit(dynamic_update_index_in_dim)/dynamic_update_slice | solution.py:134
  620.0 3.0 bitcast_add_fusion.5
  625.8 4.3 fusion.76
  633.1 56.8 %dynamic_update_slice.12 = f32[3,256,40,64]{1,0,3,2:T(4,128)} dynamic-update-slice(f32[3,256,40,64]{1,0,3,2:T(4,128)} %get-tuple-element.412, f32[1,256,40,64]{1,0,3,2:T(1,128)S(1)} %copy.76, s32[]{:T(128)} %get-tuple-element.410, s32[]{:T(128)} %constant.52.clone.1..sunk, s32[]{:T(128)} %constant.52.clone.1..sunk, s32[]{:T(128)} %constant.52.clone.1..sunk) | dynamic-update-slice | bytes 5242884 | tf_op jit(solution)/shard_map/while/body/jit(dynamic_update_index_in_dim)/dynamic_update_slice | solution.py:134
  689.8 3.0 bitcast_add_fusion.5
  692.8 5.9 copy.63
  698.8 4.3 fusion.35
  703.0 6.3 copy.51
  (112 shorter events, 70.8 us)
Async XLA Ops:
  249.3 13.2 %copy-start.1 = (f32[1,40,768]{2,1,0:T(8,128)S(1)}, f32[1,40,768]{2,1,0:T(8,128)}, u32[]{:S(2)}) copy-start(f32[1,40,768]{2,1,0:T(8,128)} %param.13) | copy-start | bytes 368644
  249.3 15.4 %copy-start.2 = (bf16[4,2816]{1,0:T(4,128)(2,1)S(1)}, bf16[4,2816]{1,0:T(4,128)(2,1)}, u32[]{:S(2)}) copy-start(bf16[4,2816]{1,0:T(4,128)(2,1)} %param.15) | copy-start | bytes 67588
  262.5 12.8 %collective-permute-start.3 = (bf16[1408,2560]{1,0:T(8,128)(2,1)}, bf16[1408,2560]{1,0:T(8,128)(2,1)}, u32[]{:S(2)}, u32[]{:S(2)}) collective-permute-start(bf16[1408,2560]{1,0:T(8,128)(2,1)} %reshape.77), channel_id=1, source_target_pairs={{0,1},{1,0},{2,3},{3,2},{4,5},{5,4},{6,7},{7,6},{8,9},{9,8},{10,11... | collective-permute-start | bytes 21626888 | tf_op jit(solution)/shard_map/ppermute | solution.py:70
  265.0 10.3 %copy-start.5 = (bf16[1,768,2560]{2,1,0:T(8,128)(2,1)S(1)}, bf16[1,768,2560]{2,1,0:T(8,128)(2,1)}, u32[]{:S(2)}) copy-start(bf16[1,768,2560]{2,1,0:T(8,128)(2,1)} %param.12) | copy-start | bytes 11796484
  305.8 16.9 %collective-permute-start.4 = (bf16[3,2816]{1,0:T(4,128)(2,1)S(1)}, bf16[3,2816]{1,0:T(4,128)(2,1)S(1)}, u32[]{:S(2)}, u32[]{:S(2)}) collective-permute-start(bf16[3,2816]{1,0:T(4,128)(2,1)S(1)} %slice.52), channel_id=1, source_target_pairs={{0,1},{1,2},{2,3},{3,4},{4,5},{5,6},{6,7},{8,9},{9,10},{10,11},{11... | collective-permute-start | bytes 50696 | tf_op jit(solution)/shard_map/ppermute | solution.py:53
  315.0 8.1 %copy-start.3 = (f32[2816]{0:T(1024)S(1)}, f32[2816]{0:T(1024)}, u32[]{:S(2)}) copy-start(f32[2816]{0:T(1024)} %param.16) | copy-start | bytes 33796
  338.5 3.3 copy-start
  372.9 18.9 %collective-permute-start.5 = (f32[40,64,128]{2,1,0:T(8,128)S(1)}, f32[40,64,128]{2,1,0:T(8,128)S(1)}, u32[]{:S(2)}, u32[]{:S(2)}) collective-permute-start(f32[40,64,128]{2,1,0:T(8,128)S(1)} %get-tuple-element.112), channel_id=1, source_target_pairs={{0,1},{1,2},{2,3},{3,4},{4,5},{5,6},{6,7},{8,9},{9,10},{10,11},{11... | collective-permute-start | bytes 3932168 | tf_op jit(solution)/shard_map/ppermute | solution.py:53
  391.9 23.8 %collective-permute-start.6 = (f32[40,64,128]{2,1,0:T(8,128)S(1)}, f32[40,64,128]{2,1,0:T(8,128)S(1)}, u32[]{:S(2)}, u32[]{:S(2)}) collective-permute-start(f32[40,64,128]{2,1,0:T(8,128)S(1)} %collective-permute-done.5), channel_id=1, source_target_pairs={{0,1},{1,2},{2,3},{3,4},{4,5},{5,6},{6,7},{8,9},{9,10},{10,11},{11... | collective-permute-start | bytes 3932168 | tf_op jit(solution)/shard_map/ppermute | solution.py:53
  393.8 17.1 %collective-permute-start = (f32[40]{0:T(128)S(1)}, f32[40]{0:T(128)S(1)}, u32[]{:S(2)}, u32[]{:S(2)}) collective-permute-start(f32[40]{0:T(128)S(1)} %get-tuple-element.177), channel_id=1, source_target_pairs={{0,1},{1,2},{2,3},{3,4},{4,5},{5,6},{6,7},{8,9},{9,10},{10,11},{11... | collective-permute-start | bytes 488 | tf_op jit(solution)/shard_map/ppermute | solution.py:53
  410.8 4.8 collective-permute-start.1
  415.7 37.3 %copy-start.4 = (f32[40]{0:T(128)S(1)}, f32[40]{0:T(128)}, u32[]{:S(2)}) copy-start(f32[40]{0:T(128)} %param.17) | copy-start | bytes 484
  415.9 30.7 %collective-permute-start.7 = (f32[40,64,128]{2,1,0:T(8,128)S(1)}, f32[40,64,128]{2,1,0:T(8,128)S(1)}, u32[]{:S(2)}, u32[]{:S(2)}) collective-permute-start(f32[40,64,128]{2,1,0:T(8,128)S(1)} %multiply_add_fusion.2), channel_id=1, source_target_pairs={{0,2},{1,3},{2,4},{3,5},{4,6},{5,7},{8,10},{9,11},{10,12},{11,13},... | collective-permute-start | bytes 3932168 | tf_op jit(solution)/shard_map/ppermute | solution.py:53
  446.9 35.2 %collective-permute-start.8 = (f32[40,64,128]{2,1,0:T(8,128)S(1)}, f32[40,64,128]{2,1,0:T(8,128)S(1)}, u32[]{:S(2)}, u32[]{:S(2)}) collective-permute-start(f32[40,64,128]{2,1,0:T(8,128)S(1)} %multiply_add_fusion.1), channel_id=1, source_target_pairs={{0,4},{1,5},{2,6},{3,7},{8,12},{9,13},{10,14},{11,15},{16,20},{17,... | collective-permute-start | bytes 3932168 | tf_op jit(solution)/shard_map/ppermute | solution.py:53
  450.8 30.1 %collective-permute-start.2 = (f32[40]{0:T(128)S(1)}, f32[40]{0:T(128)S(1)}, u32[]{:S(2)}, u32[]{:S(2)}) collective-permute-start(f32[40]{0:T(128)S(1)} %get-tuple-element.226), channel_id=1, source_target_pairs={{0,2},{1,3},{2,4},{3,5},{4,6},{5,7},{8,10},{9,11},{10,12},{11,13},... | collective-permute-start | bytes 488 | tf_op jit(solution)/shard_map/ppermute | solution.py:53
